TPU v7x, 256 devices: a whole 4x4x8 slice. The times are simulated.
256 devices in a mesh: dp: 8 (over z), tm: 32 (over x, y, core).
Axes of the slice: x: 4, y: 4, z: 8, core: 2. Of those that a mesh axis runs over, the one named last changes fastest.
Arguments:
- clips: bfloat16 [8, 128, 16, 16, 128], P('dp', 'tm'), may hold values from -6 to 6
- segment_ids: int32 [8, 128], P('dp'), may hold values from 0 to 3, never falling along the last dimension, each value on 1 to 64 neighbouring positions
- conv_weight: bfloat16 [3456, 128], replicated, may hold values from -0.109375 to 0.109375
- cotangent: bfloat16 [8, 128, 16, 16, 128], P('dp', 'tm'), may hold values from -6 to 6
Outputs:
- activated: bfloat16 [8, 128, 16, 16, 128], P('dp', 'tm')
- grad_clips: bfloat16 [8, 128, 16, 16, 128], P('dp', 'tm')
- grad_weight: float32 [3456, 128], P('tm')
Inputs may be any that keep to these rules, and one draw needn't show every extreme that they name: segment_ids never fall along a sequence; each clip has 1 to 64 frames and one has exactly that many.
All inputs are finite; a program needn't handle non-finite values.
Results may differ from a plain program's by a relative error of at most 0.013.
Values may be sent and summed in bfloat16 or wider, within the bound.
No kernel may reach another device: no remote copies, remote signals or barrier semaphores. Data moves between devices by JAX's collectives and lax.ppermute only.
A program may use at most 64 MiB of HBM per device.

v0:
```python
import jax
import jax.numpy as jnp
from jax import lax
from jax.sharding import PartitionSpec as P


def from_behind(value, axis, steps):
    count = lax.axis_size(axis)
    leading, last = (max(0, -steps), min(count, count - steps))
    return lax.ppermute(value, axis, [(source, source + steps) for source in range(leading, last)])


def per_device(clips, segment_ids, conv_weight, cotangent):
    nfr = clips.shape[1]
    hh = clips.shape[2]
    ww = clips.shape[3]
    cc = clips.shape[4]
    rows = nfr * hh * ww
    earlier = from_behind(clips[:, nfr - 2 :], "tm", 1)
    extended = jnp.concatenate([earlier, clips], axis=1)[0]
    segrow = segment_ids[0]
    segp = jnp.concatenate([jnp.full((2,), -1, jnp.int32), segrow, jnp.full((2,), -2, jnp.int32)])
    start = lax.axis_index("tm") * nfr
    seglocal = lax.dynamic_slice_in_dim(segp, start, nfr + 4, 0)
    own = seglocal[2 : 2 + nfr]
    patches = []
    pre = jnp.zeros((rows, cc), jnp.float32)
    for kt in range(3):
        moved = extended[kt : kt + nfr]
        keep = seglocal[kt : kt + nfr] == own
        moved = jnp.where(keep[:, None, None, None], moved, jnp.zeros_like(moved))
        padded = jnp.pad(moved, ((0, 0), (1, 1), (1, 1), (0, 0)))
        pieces = [padded[:, ky : ky + hh, kx : kx + ww] for ky in range(3) for kx in range(3)]
        patch = jnp.concatenate(pieces, axis=3).reshape(rows, 9 * cc)
        patches.append(patch)
        pre = pre + jnp.dot(
            patch, conv_weight[kt * 9 * cc : (kt + 1) * 9 * cc], preferred_element_type=jnp.float32
        )
    activated = jax.nn.silu(pre).astype(jnp.bfloat16).reshape(clips.shape)
    sig = jax.nn.sigmoid(pre)
    grad_pre = (
        cotangent.reshape(rows, cc).astype(jnp.float32) * sig * (1.0 + pre * (1.0 - sig))
    ).astype(jnp.bfloat16)
    count = lax.axis_size("dp") * lax.axis_size("tm") * rows
    grad_local = jnp.concatenate(
        [
            lax.dot_general(
                patch, grad_pre, (((0,), (0,)), ((), ())), preferred_element_type=jnp.float32
            )
            for patch in patches
        ],
        axis=0,
    )
    grad_local = grad_local / jnp.sqrt(jnp.float32(count))
    frames_grad = grad_pre.reshape(1, nfr, hh, ww, cc)
    later_part = from_behind(frames_grad[:, :2], "tm", -1)
    grad_ext = jnp.concatenate([frames_grad, later_part], axis=1)[0]
    summed = jnp.zeros((rows, 9 * cc), jnp.float32)
    for kt in range(3):
        d = 2 - kt
        later = grad_ext[d : d + nfr]
        keep = seglocal[2 + d : 2 + d + nfr] == own
        later = jnp.where(keep[:, None, None, None], later, jnp.zeros_like(later)).reshape(rows, cc)
        summed = summed + lax.dot_general(
            later,
            conv_weight[kt * 9 * cc : (kt + 1) * 9 * cc],
            (((1,), (1,)), ((), ())),
            preferred_element_type=jnp.float32,
        )
    summed = summed.reshape(nfr, hh, ww, 9, cc)
    canvas = jnp.zeros((nfr, hh + 2, ww + 2, cc), jnp.float32)
    for ky in range(3):
        for kx in range(3):
            canvas = canvas.at[:, ky : ky + hh, kx : kx + ww].add(summed[:, :, :, ky * 3 + kx])
    grad_clips = canvas[:, 1:-1, 1:-1].astype(jnp.bfloat16).reshape(clips.shape)
    share_rows = grad_local.shape[0] // lax.axis_size("tm")
    total = lax.psum(grad_local, ("dp", "tm"))
    grad_weight = lax.dynamic_slice_in_dim(total, lax.axis_index("tm") * share_rows, share_rows, 0)
    return (activated, grad_clips, grad_weight)


def solution(mesh):
    return jax.shard_map(
        per_device,
        mesh=mesh,
        in_specs=(
            P("dp", "tm", None, None, None),
            P("dp", None),
            P(),
            P("dp", "tm", None, None, None),
        ),
        out_specs=(P("dp", "tm", None, None, None), P("dp", "tm", None, None, None), P("tm", None)),
        check_vma=False,
    )
```

profile of v0, /device:TPU:2, one launch (start us, length us, event | category | flops | bytes accessed | tf_op | source)
XLA Modules:
  0.0 301.6 jit_solution(8584760968547292022)
XLA Ops:
  7.2 0.9 slice.482
  8.2 1.9 collective-permute-start
  11.0 2.5 pad_slice_fusion
  20.5 1.6 fusion.3
  22.9 0.8 fusion.36
  23.7 0.8 fusion.35
  24.6 5.8 %collective-permute-start.1 = (bf16[1,2,16,16,128]{4,3,2,1,0:T(8,128)(2,1)S(1)}, bf16[1,2,16,16,128]{4,3,2,1,0:T(8,128)(2,1)S(1)}, u32[]{:S(2)}, u32[]{:S(2)}) collective-permute-start(bf16[1,2,16,16,128]{4,3,2,1,0:T(8,128)(2,1)S(1)} %slice.545), channel_id=1, source_target_pairs={{1,0},{2,1},{3,2},{4,3},{5,4},{6,5},{7,6},{8,7},{9,8},{10,9},{11,1... | collective-permute-start | bytes 393224 | tf_op jit(solution)/shard_map/ppermute | solution.py:10
  30.4 1.3 maximum_multiply_fusion
  31.7 1.0 collective-permute-done.1
  34.7 3.0 convolution_add_fusion
  37.7 6.9 %reshape.439 = f32[4,16,16,9,128]{4,3,2,1,0:T(8,128)} reshape(f32[1024,1152]{1,0:T(8,128)} %convolution_add_fusion) | data formatting | bytes 9437184 | tf_op jit(solution)/shard_map/reshape | solution.py:70
  44.6 16.6 %fusion.32 = (f32[4,16,16,1,128]{4,3,2,1,0:T(1,128)S(1)}, f32[4,16,16,1,128]{4,3,2,1,0:T(1,128)S(1)}, f32[4,16,16,1,128]{4,3,2,1,0:T(1,128)S(1)}, f32[4,16,16,1,...) fusion(f32[4,16,16,9,128]{4,3,2,1,0:T(8,128)} %reshape.439), kind=kLoop, calls=%fused_computation.101 | loop fusion | bytes 9437184 | tf_op jit(solution)/shard_map/slice | solution.py:74
  61.2 2.2 dynamic-slice_add_fusion
  63.4 4.3 %scatter-add.31 = f32[4,18,18,128]{3,2,1,0:T(8,128)S(1)} dynamic-update-slice(f32[4,18,18,128]{3,2,1,0:T(8,128)S(1)} %scatter-add.30, f32[4,16,16,128]{3,2,1,0:T(8,128)} %dynamic-slice_add_fusion, s32[]{:T(128)} %constant.283.clone.1, s32[]{:T(128)} %bitcast.21, s32[]{:T(128)} %bitcast.22, s32[]{:T(128)} %constant.283.clone.1) | dynamic-update-slice | bytes 1048580 | tf_op jit(solution)/shard_map/scatter-add | solution.py:74
  67.7 3.8 %add_select_fusion = f32[4,16,16,128]{3,2,1,0:T(8,128)} fusion(f32[4,16,16,128]{3,2,1,0:T(8,128)} %bitcast.89, f32[4,18,18,128]{3,2,1,0:T(8,128)S(1)} %scatter-add.31, s32[]{:T(128)} %bitcast.24, s32[]{:T(128)} %bitcast.25, pred[]{:T(512)} %and_reduce_fusion), kind=kLoop, calls=%fused_computation.5 | loop fusion | flops 262144 | bytes 1572873 | tf_op jit(solution)/shard_map/select.11
  71.5 4.3 %scatter-add.34 = f32[4,18,18,128]{3,2,1,0:T(8,128)S(1)} dynamic-update-slice(f32[4,18,18,128]{3,2,1,0:T(8,128)S(1)} %scatter-add.31, f32[4,16,16,128]{3,2,1,0:T(8,128)} %add_select_fusion, s32[]{:T(128)} %constant.283.clone.1, s32[]{:T(128)} %bitcast.24, s32[]{:T(128)} %bitcast.25, s32[]{:T(128)} %constant.283.clone.1) | dynamic-update-slice | bytes 1048580 | tf_op jit(solution)/shard_map/scatter-add | solution.py:74
  75.8 1.1 fusion.1
  77.0 0.9 slice_add_fusion.4
  77.9 3.0 %scatter-add.36 = f32[4,18,18,128]{3,2,1,0:T(8,128)S(1)} dynamic-update-slice(f32[4,18,18,128]{3,2,1,0:T(8,128)S(1)} %fusion.1, f32[4,16,16,128]{3,2,1,0:T(8,128)} %slice_add_fusion.4, s32[]{:T(128)} %constant.283.clone.1, s32[]{:T(128)} %constant.292.clone.1, s32[]{:T(128)} %constant.292.clone.1, s32[]{:T(128)} %constant.283.clone.1) | dynamic-update-slice | bytes 1048580 | tf_op jit(solution)/shard_map/scatter-add | solution.py:74
  81.0 1.7 scatter-add.39
  82.8 1.7 scatter-add.41
  84.6 1.7 scatter-add.44
  87.0 206.2 %all-reduce.6.cloned.1.call-done = f32[3456,128]{1,0:T(8,128)} async-done(((f32[3456,128]{1,0:T(8,128)}), f32[3456,128]{1,0:T(8,128)}) %all-reduce.6.cloned.1.call-update) | async-done | bytes 1769488 | tf_op jit(solution)/shard_map/psum | solution.py:77
  293.3 1.5 constant_dynamic-slice_fusion
  (69 shorter events, 11.6 us)
Async XLA Ops:
  7.2 7.2 %copy-start = (bf16[1,4,16,16,128]{4,3,2,1,0:T(8,128)(2,1)S(1)}, bf16[1,4,16,16,128]{4,3,2,1,0:T(8,128)(2,1)}, u32[]{:S(2)}) copy-start(bf16[1,4,16,16,128]{4,3,2,1,0:T(8,128)(2,1)} %param.22) | copy-start | bytes 786436
  7.2 286.1 %all-reduce.6.cloned.1.call-start = ((), (), s32[]{:S(2)}) async-start(), calls=%async_computation | async-start | bytes 3538944 | tf_op jit(solution)/shard_map/psum | solution.py:77
  8.2 8.4 %collective-permute-start = (bf16[1,2,16,16,128]{4,3,2,1,0:T(8,128)(2,1)S(1)}, bf16[1,2,16,16,128]{4,3,2,1,0:T(8,128)(2,1)S(1)}, u32[]{:S(2)}, u32[]{:S(2)}) collective-permute-start(bf16[1,2,16,16,128]{4,3,2,1,0:T(8,128)(2,1)S(1)} %slice.482), channel_id=1, source_target_pairs={{0,1},{1,2},{2,3},{3,4},{4,5},{5,6},{6,7},{7,8},{8,9},{9,10},{10,1... | collective-permute-start | bytes 393224 | tf_op jit(solution)/shard_map/ppermute | solution.py:10
  13.5 1.2 copy-start.2
  17.6 1.2 copy-start.1
  19.5 1.0 copy-start.3
  24.6 8.1 %collective-permute-start.1 = (bf16[1,2,16,16,128]{4,3,2,1,0:T(8,128)(2,1)S(1)}, bf16[1,2,16,16,128]{4,3,2,1,0:T(8,128)(2,1)S(1)}, u32[]{:S(2)}, u32[]{:S(2)}) collective-permute-start(bf16[1,2,16,16,128]{4,3,2,1,0:T(8,128)(2,1)S(1)} %slice.545), channel_id=1, source_target_pairs={{1,0},{2,1},{3,2},{4,3},{5,4},{6,5},{7,6},{8,7},{9,8},{10,9},{11,1... | collective-permute-start | bytes 393224 | tf_op jit(solution)/shard_map/ppermute | solution.py:10
Sparse Core Ops, SparseCore 0:
  31.9 261.3 all-reduce.5
where the time goes:
time: 302 us
  waiting for transfers between devices  207 us (69%)
  local copies, waits for them, and re-layouts  50.1 us (17%)
  between operations  14.5 us (5%)
  other arithmetic  11.7 us (4%)
  matrix products  10.2 us (3%)
  starting transfers between devices  7.76 us (3%)
    psum x1, waiting for transfers between devices, per_device(): total = lax.psum(grad_local, ('dp', 'tm'))  206 us
    scatter-add x7, local copies, waits for them, and re-layouts, per_device(): canvas.at[:, ky:ky + hh, kx:kx + ww].add(summed[:, :, :, ky * 3 + kx])  16.8 us
    slice x1, local copies, waits for them, and re-layouts, per_device(): summed[:, :, :, ky * 3 + kx]  16.6 us
    ppermute x2, starting transfers between devices, from_behind(): lax.ppermute(value, axis, [(source, source + steps) for source in range(l...  7.72 us
    reshape x1, local copies, waits for them, and re-layouts, per_device(): summed = summed.reshape(nfr, hh, ww, 9, cc)  6.85 us
  transfers between devices with their start and end apart: 3, of which 3 were waited for; matrix products, arithmetic and copies ran while one was open for 20% of the time, Pallas kernels for 0%

commit v1 on v0

--- a/solution.py
+++ b/solution.py
@@ -74,7 +74,7 @@
             canvas = canvas.at[:, ky : ky + hh, kx : kx + ww].add(summed[:, :, :, ky * 3 + kx])
     grad_clips = canvas[:, 1:-1, 1:-1].astype(jnp.bfloat16).reshape(clips.shape)
     share_rows = grad_local.shape[0] // lax.axis_size("tm")
-    total = lax.psum(grad_local, ("dp", "tm"))
+    total = lax.psum(lax.psum(grad_local, "tm"), "dp")
     grad_weight = lax.dynamic_slice_in_dim(total, lax.axis_index("tm") * share_rows, share_rows, 0)
     return (activated, grad_clips, grad_weight)
 

time: 302 us -> 240 us (0.79)
  waiting for transfers between devices: 207 us -> 145 us
    psum x1 -> x2, waiting for transfers between devices: 206 us -> 144 us  [per_device(): total = lax.psum(lax.psum(grad_local, 'tm'), 'dp')]
  transfers between devices with their start and end apart: 3 -> 4, of which waited for: 3 -> 4; matrix products, arithmetic and copies ran while one was open for 20% -> 26% of each run, Pallas kernels for 0% -> 0%
where the time goes in v1:
time: 240 us; the launch traced here: 239 us
  waiting for transfers between devices  145 us (60%)
  local copies, waits for them, and re-layouts  50.1 us (21%)
  between operations  14.5 us (6%)
  other arithmetic  11.7 us (5%)
  matrix products  10.2 us (4%)
  starting transfers between devices  7.8 us (3%)
    psum x2, waiting for transfers between devices, per_device(): total = lax.psum(lax.psum(grad_local, 'tm'), 'dp')  144 us
    scatter-add x7, local copies, waits for them, and re-layouts, per_device(): canvas.at[:, ky:ky + hh, kx:kx + ww].add(summed[:, :, :, ky * 3 + kx])  16.8 us
    slice x1, local copies, waits for them, and re-layouts, per_device(): summed[:, :, :, ky * 3 + kx]  16.6 us
    ppermute x2, starting transfers between devices, from_behind(): lax.ppermute(value, axis, [(source, source + steps) for source in range(l...  7.54 us
    reshape x1, local copies, waits for them, and re-layouts, per_device(): summed = summed.reshape(nfr, hh, ww, 9, cc)  6.85 us
  transfers between devices with their start and end apart: 4, of which 4 were waited for; matrix products, arithmetic and copies ran while one was open for 26% of the time, Pallas kernels for 0%

profile of v1, /device:TPU:2, one launch (start us, length us, event | category | flops | bytes accessed | tf_op | source)
XLA Modules:
  0.0 239.1 jit_solution(17300621908931000470)
XLA Ops:
  7.2 0.9 slice.482
  8.2 1.9 collective-permute-start
  11.0 2.5 %pad_slice_fusion = (bf16[4,16,16,128]{3,2,1,0:T(8,128)(2,1)S(1)}, bf16[4,16,16,128]{3,2,1,0:T(8,128)(2,1)S(1)}, bf16[4,16,16,128]{3,2,1,0:T(8,128)(2,1)S(1)}, b...) fusion(bf16[4,16,16,128]{3,2,1,0:T(8,128)(2,1)} %bitcast.81), kind=kLoop, calls=%fused_computation.6 | loop fusion | bytes 2359296 | tf_op jit(solution)/shard_map/slice | solution.py:33
  20.5 1.6 fusion.3
  23.7 0.8 fusion.35
  24.6 5.6 %collective-permute-start.1 = (bf16[1,2,16,16,128]{4,3,2,1,0:T(8,128)(2,1)S(1)}, bf16[1,2,16,16,128]{4,3,2,1,0:T(8,128)(2,1)S(1)}, u32[]{:S(2)}, u32[]{:S(2)}) collective-permute-start(bf16[1,2,16,16,128]{4,3,2,1,0:T(8,128)(2,1)S(1)} %slice.545), channel_id=1, source_target_pairs={{1,0},{2,1},{3,2},{4,3},{5,4},{6,5},{7,6},{8,7},{9,8},{10,9},{11,1... | collective-permute-start | bytes 393224 | tf_op jit(solution)/shard_map/ppermute | solution.py:10
  30.2 1.3 maximum_multiply_fusion
  31.8 0.9 collective-permute-done.1
  34.7 3.0 %convolution_add_fusion = f32[1024,1152]{1,0:T(8,128)} fusion(f32[1024,1152]{1,0:T(8,128)S(1)} %convolution_add_fusion.1, bf16[1024,128]{1,0:T(8,128)(2,1)S(1)} %get-tuple-element.120, bf16[3456,128]{1,0:T(8,128)(2,1)S(1)} %copy-done.1), kind=kOutput, calls=%fused_computation | convolution fusion | flops 303169536 | bytes 9994240 | tf_op jit(solution)/shard_map/dot_general | solution.py:64
  37.7 6.9 %reshape.439 = f32[4,16,16,9,128]{4,3,2,1,0:T(8,128)} reshape(f32[1024,1152]{1,0:T(8,128)} %convolution_add_fusion) | data formatting | bytes 9437184 | tf_op jit(solution)/shard_map/reshape | solution.py:70
  44.6 16.6 %fusion.32 = (f32[4,16,16,1,128]{4,3,2,1,0:T(1,128)S(1)}, f32[4,16,16,1,128]{4,3,2,1,0:T(1,128)S(1)}, f32[4,16,16,1,128]{4,3,2,1,0:T(1,128)S(1)}, f32[4,16,16,1,...) fusion(f32[4,16,16,9,128]{4,3,2,1,0:T(8,128)} %reshape.439), kind=kLoop, calls=%fused_computation.101 | loop fusion | bytes 9437184 | tf_op jit(solution)/shard_map/slice | solution.py:74
  61.2 2.2 dynamic-slice_add_fusion
  63.4 4.3 %scatter-add.31 = f32[4,18,18,128]{3,2,1,0:T(8,128)S(1)} dynamic-update-slice(f32[4,18,18,128]{3,2,1,0:T(8,128)S(1)} %scatter-add.30, f32[4,16,16,128]{3,2,1,0:T(8,128)} %dynamic-slice_add_fusion, s32[]{:T(128)} %constant.283.clone.1, s32[]{:T(128)} %bitcast.21, s32[]{:T(128)} %bitcast.22, s32[]{:T(128)} %constant.283.clone.1) | dynamic-update-slice | bytes 1048580 | tf_op jit(solution)/shard_map/scatter-add | solution.py:74
  67.7 3.8 %add_select_fusion = f32[4,16,16,128]{3,2,1,0:T(8,128)} fusion(f32[4,16,16,128]{3,2,1,0:T(8,128)} %bitcast.89, f32[4,18,18,128]{3,2,1,0:T(8,128)S(1)} %scatter-add.31, s32[]{:T(128)} %bitcast.24, s32[]{:T(128)} %bitcast.25, pred[]{:T(512)} %and_reduce_fusion), kind=kLoop, calls=%fused_computation.5 | loop fusion | flops 262144 | bytes 1572873 | tf_op jit(solution)/shard_map/select.11
  71.5 4.3 %scatter-add.34 = f32[4,18,18,128]{3,2,1,0:T(8,128)S(1)} dynamic-update-slice(f32[4,18,18,128]{3,2,1,0:T(8,128)S(1)} %scatter-add.31, f32[4,16,16,128]{3,2,1,0:T(8,128)} %add_select_fusion, s32[]{:T(128)} %constant.283.clone.1, s32[]{:T(128)} %bitcast.24, s32[]{:T(128)} %bitcast.25, s32[]{:T(128)} %constant.283.clone.1) | dynamic-update-slice | bytes 1048580 | tf_op jit(solution)/shard_map/scatter-add | solution.py:74
  75.8 72.3 %all-reduce.7.cloned.1.call-done = f32[3456,128]{1,0:T(8,128)} async-done(((f32[3456,128]{1,0:T(8,128)}), f32[3456,128]{1,0:T(8,128)}) %all-reduce.7.cloned.1.call-update) | async-done | bytes 1769488 | tf_op jit(solution)/shard_map/psum | solution.py:77
  148.2 1.1 fusion.1
  149.3 0.9 slice_add_fusion.4
  150.2 3.0 %scatter-add.36 = f32[4,18,18,128]{3,2,1,0:T(8,128)S(1)} dynamic-update-slice(f32[4,18,18,128]{3,2,1,0:T(8,128)S(1)} %fusion.1, f32[4,16,16,128]{3,2,1,0:T(8,128)} %slice_add_fusion.4, s32[]{:T(128)} %constant.283.clone.1, s32[]{:T(128)} %constant.292.clone.1, s32[]{:T(128)} %constant.292.clone.1, s32[]{:T(128)} %constant.283.clone.1) | dynamic-update-slice | bytes 1048580 | tf_op jit(solution)/shard_map/scatter-add | solution.py:74
  153.3 1.7 scatter-add.39
  155.2 1.7 scatter-add.41
  156.9 1.7 scatter-add.44
  159.4 71.5 %all-reduce.9.cloned.1.call-done = f32[3456,128]{1,0:T(8,128)} async-done(((f32[3456,128]{1,0:T(8,128)}), f32[3456,128]{1,0:T(8,128)}) %all-reduce.9.cloned.1.call-update) | async-done | bytes 1769488 | tf_op jit(solution)/shard_map/psum | solution.py:77
  230.8 1.5 constant_dynamic-slice_fusion
  (72 shorter events, 12.7 us)
Async XLA Ops:
  7.2 7.2 %copy-start = (bf16[1,4,16,16,128]{4,3,2,1,0:T(8,128)(2,1)S(1)}, bf16[1,4,16,16,128]{4,3,2,1,0:T(8,128)(2,1)}, u32[]{:S(2)}) copy-start(bf16[1,4,16,16,128]{4,3,2,1,0:T(8,128)(2,1)} %param.22) | copy-start | bytes 786436
  7.2 141.0 %all-reduce.7.cloned.1.call-start = ((), (), s32[]{:S(2)}) async-start(), calls=%async_computation | async-start | bytes 3538944 | tf_op jit(solution)/shard_map/psum | solution.py:77
  8.2 8.4 %collective-permute-start = (bf16[1,2,16,16,128]{4,3,2,1,0:T(8,128)(2,1)S(1)}, bf16[1,2,16,16,128]{4,3,2,1,0:T(8,128)(2,1)S(1)}, u32[]{:S(2)}, u32[]{:S(2)}) collective-permute-start(bf16[1,2,16,16,128]{4,3,2,1,0:T(8,128)(2,1)S(1)} %slice.482), channel_id=1, source_target_pairs={{0,1},{1,2},{2,3},{3,4},{4,5},{5,6},{6,7},{7,8},{8,9},{9,10},{10,1... | collective-permute-start | bytes 393224 | tf_op jit(solution)/shard_map/ppermute | solution.py:10
  13.5 1.2 copy-start.2
  17.6 1.2 copy-start.1
  19.5 1.0 copy-start.3
  24.6 8.1 %collective-permute-start.1 = (bf16[1,2,16,16,128]{4,3,2,1,0:T(8,128)(2,1)S(1)}, bf16[1,2,16,16,128]{4,3,2,1,0:T(8,128)(2,1)S(1)}, u32[]{:S(2)}, u32[]{:S(2)}) collective-permute-start(bf16[1,2,16,16,128]{4,3,2,1,0:T(8,128)(2,1)S(1)} %slice.545), channel_id=1, source_target_pairs={{1,0},{2,1},{3,2},{4,3},{5,4},{6,5},{7,6},{8,7},{9,8},{10,9},{11,1... | collective-permute-start | bytes 393224 | tf_op jit(solution)/shard_map/ppermute | solution.py:10
  31.6 199.3 %all-reduce.9.cloned.1.call-start = ((), (), s32[]{:S(2)}) async-start(), calls=%async_computation.1 | async-start | bytes 3538944 | tf_op jit(solution)/shard_map/psum | solution.py:77
Sparse Core Ops, SparseCore 0:
  31.7 116.4 all-reduce.6
  150.5 80.2 all-reduce.8
